TPU v7x, 256 devices: a whole 4x4x8 slice. The times are simulated.
256 devices in a mesh: ctx: 16 (over z_lo, x), ch: 16 (over y, z_hi, core).
Axes of the slice: x: 4, y: 4, z: 8 (z_hi: 2, z_lo: 4; z = z_hi * 4 + z_lo), core: 2. Of those that a mesh axis runs over, the one named last changes fastest.
Arguments:
- tokens: bfloat16 [4096, 8192], P('ctx', 'ch'), may hold values from -6 to 6
- in_weight: bfloat16 [8192, 3, 8192], P('ctx', None, 'ch'), may hold values from -0.0625 to 0.0625
- short_filter: bfloat16 [3, 3, 8192], P(None, None, 'ch'), may hold values from -3 to 3
- decay_rate: float32 [8192, 16], P('ch'), may hold values from 1.2207031e-05 to 0.0333333333
- residue: float32 [8192, 16], P('ch'), may hold values from -0.12 to 0.12
- skip_gain: float32 [8192], P('ch'), may hold values from -4 to 4
Outputs:
- filtered: bfloat16 [4096, 8192], P('ctx', 'ch')
All inputs are finite; a program needn't handle non-finite values.
Results may differ from a plain program's by a relative error of at most 0.007.
Values may be sent and summed in bfloat16 or wider, within the bound.
No kernel may reach another device: no remote copies, remote signals or barrier semaphores. Data moves between devices by JAX's collectives and lax.ppermute only.
A program may use at most 128 MiB of HBM per device.

v0:
```python
import jax
import jax.numpy as jnp
import numpy as np
from jax import lax
from jax.sharding import Mesh, PartitionSpec as P

exact_mode = lax.Precision.HIGHEST
SEQ = ("zl", "x")


def from_behind(block, axis, distance):
    devices = range(lax.axis_size(axis))
    route = [(i - distance, i) for i in devices if i - distance in devices]
    return lax.ppermute(block, axis, route)


def ring_sends(pieces, axis, size):
    position = lax.axis_index(axis)
    received = []
    for k in range(1, size):
        route = [(i, (i + k) % size) for i in range(size)]
        received.append(lax.ppermute(pieces(k, position), axis, route))
    return received


def local(tokens, in_weight, short_filter, decay_rate, residue, skip_gain):
    tok_rows = tokens.shape[0]
    width_local = in_weight.shape[2]
    mode_count = decay_rate.shape[1]
    feat_block = in_weight.shape[0]
    across, down = (lax.axis_size("x"), lax.axis_size("zl"))
    me_x, me_z = (lax.axis_index("x"), lax.axis_index("zl"))
    flat_own = in_weight.reshape(feat_block, 3 * width_local)
    weights = [flat_own] + ring_sends(lambda k, p: flat_own, "x", across)
    gathered = lax.all_gather(tokens, "ch", axis=1, tiled=True)
    chunk = gathered.shape[1] // down

    def chunk_for(k, p):
        return lax.dynamic_slice_in_dim(gathered, (p + k) % down * chunk, chunk, axis=1)

    rows = [chunk_for(0, me_z)] + ring_sends(chunk_for, "zl", down)
    column = jnp.concatenate(rows, axis=0)
    partial = jnp.zeros((column.shape[0], 3 * width_local), jnp.float32)
    for k in range(across):
        source = (me_x - k) % across
        taken = lax.dynamic_slice_in_dim(column, source * feat_block, feat_block, axis=1)
        partial = partial + jnp.dot(taken, weights[k], preferred_element_type=jnp.float32)
    pieces = partial.reshape(down, tok_rows, 3 * width_local)
    projected = pieces[0]
    for k in range(1, down):
        route = [(i, (i - k) % down) for i in range(down)]
        back = lax.ppermute(pieces[k].astype(jnp.bfloat16), "zl", route)
        projected = projected + back.astype(jnp.float32)
    streams = projected.astype(jnp.bfloat16).reshape(tok_rows, 3, width_local)
    tap_count = short_filter.shape[0]
    last_rows = streams[tok_rows - (tap_count - 1) :]
    before = from_behind(last_rows, SEQ, 1)
    padded = jnp.concatenate([before, streams], axis=0).astype(jnp.float32)
    filter_taps = short_filter.astype(jnp.float32)
    featured = jnp.zeros((tok_rows, 3, width_local), jnp.float32)
    for shift_back in range(tap_count):
        begin = tap_count - 1 - shift_back
        featured = featured + filter_taps[shift_back][None] * padded[begin : begin + tok_rows]
    query_gate = featured[:, 0]
    gated_rows = (featured[:, 1] * featured[:, 2]).astype(jnp.bfloat16)
    gated_wide = gated_rows.astype(jnp.float32)
    position = jnp.arange(tok_rows, dtype=jnp.float32)
    powers = jnp.exp(-decay_rate[None, :, :] * (tok_rows - 1.0 - position)[:, None, None])
    local_state = jnp.einsum("jc,jcr->cr", gated_wide, powers, precision=exact_mode)
    along = [local_state] + ring_sends(lambda k, p: local_state, "x", across)
    row = jnp.stack(along)
    states = jnp.stack([row] + ring_sends(lambda k, p: row, "zl", down))
    step_z = jnp.arange(down)[:, None]
    step_x = jnp.arange(across)[None, :]
    source = (me_z - step_z) % down * across + (me_x - step_x) % across
    lag = (me_z * across + me_x - 1 - source).astype(jnp.float32)
    decay_b = decay_rate[None, None]
    weight = jnp.exp(-decay_b * (float(tok_rows) * jnp.maximum(lag, 0.0))[:, :, None, None])
    weight = jnp.where((lag >= 0)[:, :, None, None], weight, 0.0)
    incoming = jnp.sum(weight * states, axis=(0, 1))
    growth = jnp.exp(decay_rate[None, :, :] * position[:, None, None])
    scaled = (gated_wide[:, :, None] * growth).reshape(tok_rows, width_local * mode_count)
    lower_mask = (jnp.arange(tok_rows)[:, None] >= jnp.arange(tok_rows)[None, :]).astype(
        jnp.float32
    )
    running_sum = jnp.dot(lower_mask, scaled, precision=exact_mode).reshape(
        tok_rows, width_local, mode_count
    )
    shrink = jnp.exp(-decay_rate[None, :, :] * position[:, None, None])
    entering = (incoming * jnp.exp(-decay_rate))[None]
    convolved = jnp.sum(residue[None] * shrink * (running_sum + entering), axis=2)
    long_mix = convolved + skip_gain[None, :] * gated_wide
    return (query_gate * long_mix).astype(jnp.bfloat16)


def split_mesh(mesh):
    ctx, ch = (mesh.shape["ctx"], mesh.shape["ch"])
    inner = 4 if ctx % 4 == 0 else 1
    devices = np.asarray(mesh.devices).reshape(ctx // inner, inner, ch)
    return Mesh(devices, ("zl", "x", "ch"))


def solution(mesh):
    fine = split_mesh(mesh)
    in_specs = (
        P(SEQ, "ch"),
        P(SEQ, None, "ch"),
        P(None, None, "ch"),
        P("ch", None),
        P("ch", None),
        P("ch"),
    )
    out_specs = P(SEQ, "ch")
    return jax.shard_map(local, mesh=fine, in_specs=in_specs, out_specs=out_specs, check_vma=False)
```

profile of v0, /device:TPU:32, one launch (start us, length us, event | category | flops | bytes accessed | tf_op | source)
XLA Modules:
  0.0 327.1 jit_solution(8033702825253924592)
XLA Ops:
  7.3 82.0 %all-gather.2.cloned.1.call-done = bf16[256,8192]{1,0:T(8,128)(2,1)} async-done(((bf16[256,512]{1,0:T(8,128)(2,1)}), bf16[256,8192]{1,0:T(8,128)(2,1)}) %all-gather.2.cloned.1.call-update) | async-done | bytes 4194320 | tf_op jit(solution)/shard_map/all_gather | solution.py:35
  89.3 4.1 %constant_dynamic-slice_fusion.3 = (bf16[256,2048]{1,0:T(8,128)(2,1)S(1)}, bf16[256,2048]{1,0:T(8,128)(2,1)}, bf16[256,2048]{1,0:T(8,128)(2,1)}, bf16[256,2048]{1,0:T(8,128)(2,1)}) fusion(bf16[256,8192]{1,0:T(8,128)(2,1)} %all-gather.2.cloned.1.call-done, s32[]{:T(128)S(6)} %select_n.86, s32[]{:T(128)S(6)} %select_n.92, s32[]{:T(128)S(6)} %select_n.90, ...), kind=kLoop, calls=%fused_computation.55 | loop fusion | bytes 8388624 | tf_op jit(solution)/shard_map/dynamic_slice | solution.py:39
  93.7 2.9 collective-permute-start.1
  96.9 1.6 copy.17
  99.9 2.7 collective-permute-start.4
  102.6 17.1 %collective-permute-done = bf16[256,2048]{1,0:T(8,128)(2,1)} collective-permute-done((bf16[256,2048]{1,0:T(8,128)(2,1)}, bf16[256,2048]{1,0:T(8,128)(2,1)}, u32[]{:S(2)}, u32[]{:S(2)}) %collective-permute-start) | collective-permute-done | bytes 1048608 | tf_op jit(solution)/shard_map/ppermute | solution.py:22
  119.7 2.7 collective-permute-start.5
  122.4 61.9 %collective-permute-done.1 = bf16[256,2048]{1,0:T(8,128)(2,1)} collective-permute-done((bf16[256,2048]{1,0:T(8,128)(2,1)}, bf16[256,2048]{1,0:T(8,128)(2,1)}, u32[]{:S(2)}, u32[]{:S(2)}) %collective-permute-start.1) | collective-permute-done | bytes 1048608 | tf_op jit(solution)/shard_map/ppermute | solution.py:22
  184.2 3.4 %collective-permute-done.2 = bf16[256,2048]{1,0:T(8,128)(2,1)} collective-permute-done((bf16[256,2048]{1,0:T(8,128)(2,1)}, bf16[256,2048]{1,0:T(8,128)(2,1)}, u32[]{:S(2)}, u32[]{:S(2)}) %collective-permute-start.2) | collective-permute-done | bytes 1048608 | tf_op jit(solution)/shard_map/ppermute | solution.py:22
  187.6 2.1 pad_maximum_fusion
  190.0 1.8 fusion.17
  191.8 5.9 %fusion.15 = f32[1024,1536]{1,0:T(8,128)} fusion(bf16[512,1536]{0,1:T(8,128)(2,1)} %collective-permute-done.3, bf16[1024,2048]{1,0:T(8,128)(2,1)S(1)} %pad_maximum_fusion, s32[]{:T(128)S(6)} %select_n.96), kind=kOutput, calls=%fused_computation.20 | convolution fusion | flops 1610612736 | bytes 8912900 | tf_op jit(solution)/shard_map/dot_general | solution.py:47
  197.7 4.4 %fusion.13 = f32[1024,1536]{1,0:T(8,128)} fusion(bf16[512,1536]{0,1:T(8,128)(2,1)S(1)} %collective-permute-done.4, bf16[1024,2048]{1,0:T(8,128)(2,1)S(1)} %pad_maximum_fusion, s32[]{:T(128)S(6)} %select_n.98), kind=kOutput, calls=%fused_computation.18 | convolution fusion | flops 1610612736 | bytes 8912900 | tf_op jit(solution)/shard_map/dot_general | solution.py:47
  202.1 7.4 %fusion.35 = (bf16[1024,1536]{1,0:T(8,128)(2,1)S(1)}, f32[1024,1536]{1,0:T(8,128)S(1)}) fusion(bf16[512,1536]{0,1:T(8,128)(2,1)} %collective-permute-done.5, bf16[1024,2048]{1,0:T(8,128)(2,1)S(1)} %pad_maximum_fusion, s32[]{:T(128)S(6)} %select_n.100, f32[1024,1536]{1,0:T(8,128)} %fusion.13, f32[1024,1536]{1,0:T(8,128)S(1)} %fusion.17, f32[1024,1536]{1,0:T(8,128)} %fusion.15), kind=kOutput, calls=%fused_computation.64 | convolution fusion | flops 1616904192 | bytes 30932996 | tf_op jit(solution)/shard_map/dot_general | solution.py:47
  211.0 1.9 collective-permute-start.8
  212.9 51.2 %collective-permute-done.6 = bf16[256,1536]{1,0:T(8,128)(2,1)S(1)} collective-permute-done((bf16[256,1536]{1,0:T(8,128)(2,1)S(1)}, bf16[256,1536]{1,0:T(8,128)(2,1)S(1)}, u32[]{:S(2)}, u32[]{:S(2)}) %collective-permute-start.6) | collective-permute-done | bytes 786464 | tf_op jit(solution)/shard_map/ppermute | solution.py:52
  264.1 13.7 %collective-permute-done.8 = bf16[256,1536]{1,0:T(8,128)(2,1)S(1)} collective-permute-done((bf16[256,1536]{1,0:T(8,128)(2,1)S(1)}, bf16[256,1536]{1,0:T(8,128)(2,1)S(1)}, u32[]{:S(2)}, u32[]{:S(2)}) %collective-permute-start.8) | collective-permute-done | bytes 786464 | tf_op jit(solution)/shard_map/ppermute | solution.py:52
  278.2 3.4 %collective-permute-start.9 = (bf16[2,3,512]{2,0,1:T(2,128)(2,1)S(1)}, bf16[2,3,512]{2,0,1:T(2,128)(2,1)S(1)}, u32[]{:S(2)}, u32[]{:S(2)}) collective-permute-start(bf16[2,3,512]{2,0,1:T(2,128)(2,1)S(1)} %bitcast.57), channel_id=1, source_target_pairs={{0,16},{16,32},{32,48},{48,64},{64,80},{80,96},{96,112},{112,128},... | collective-permute-start | bytes 18440 | tf_op jit(solution)/shard_map/ppermute | solution.py:14
  282.2 5.2 %collective-permute-done.9 = bf16[2,3,512]{2,0,1:T(2,128)(2,1)S(1)} collective-permute-done((bf16[2,3,512]{2,0,1:T(2,128)(2,1)S(1)}, bf16[2,3,512]{2,0,1:T(2,128)(2,1)S(1)}, u32[]{:S(2)}, u32[]{:S(2)}) %collective-permute-start.9) | collective-permute-done | bytes 6176 | tf_op jit(solution)/shard_map/ppermute | solution.py:14
  290.5 2.5 collective-permute-start.12
  297.2 3.0 collective-permute-start.14
  301.8 2.8 collective-permute-done.13
  306.1 2.1 collective-permute-done.15
  309.3 10.1 %multiply_reduce_fusion.1 = f32[256,512]{1,0:T(8,128)S(1)} fusion(f32[512,16]{0,1:T(8,128)S(1)} %exponential_multiply_fusion, f32[512,16]{0,1:T(8,128)S(1)} %neg.8, f32[512,16]{0,1:T(8,128)S(1)} %copy-done.5, f32[512,16,256]{2,1,0:T(8,128)S(1)} %bitcast.45), kind=kOutput, calls=%fused_computation.4 | convolution fusion | flops 6452871168 | bytes 9011200 | tf_op jit(solution)/shard_map/dot_general | solution.py:86
  (56 shorter events, 17.5 us)
Async XLA Ops:
  6.5 82.7 %all-gather.2.cloned.1.call-start = ((), (), s32[]{:S(2)}) async-start(), calls=%async_computation | async-start | bytes 4456448 | tf_op jit(solution)/shard_map/all_gather | solution.py:35
  7.3 89.5 %copy-start = (bf16[512,3,512]{2,0,1:T(8,128)(2,1)S(1)}, bf16[512,3,512]{2,0,1:T(8,128)(2,1)}, u32[]{:S(2)}) copy-start(bf16[512,3,512]{2,0,1:T(8,128)(2,1)} %param.7) | copy-start | bytes 4718596
  93.3 26.3 %collective-permute-start = (bf16[256,2048]{1,0:T(8,128)(2,1)}, bf16[256,2048]{1,0:T(8,128)(2,1)}, u32[]{:S(2)}, u32[]{:S(2)}) collective-permute-start(bf16[256,2048]{1,0:T(8,128)(2,1)} %get-tuple-element.10), channel_id=1, source_target_pairs={{0,64},{64,128},{128,192},{192,0},{1,65},{65,129},{129,193},{193,1... | collective-permute-start | bytes 3145736 | tf_op jit(solution)/shard_map/ppermute | solution.py:22
  93.7 90.6 %collective-permute-start.1 = (bf16[256,2048]{1,0:T(8,128)(2,1)}, bf16[256,2048]{1,0:T(8,128)(2,1)}, u32[]{:S(2)}, u32[]{:S(2)}) collective-permute-start(bf16[256,2048]{1,0:T(8,128)(2,1)} %get-tuple-element.9), channel_id=1, source_target_pairs={{0,128},{64,192},{128,0},{192,64},{1,129},{65,193},{129,1},{193,65... | collective-permute-start | bytes 3145736 | tf_op jit(solution)/shard_map/ppermute | solution.py:22
  96.6 91.0 %collective-permute-start.2 = (bf16[256,2048]{1,0:T(8,128)(2,1)}, bf16[256,2048]{1,0:T(8,128)(2,1)}, u32[]{:S(2)}, u32[]{:S(2)}) collective-permute-start(bf16[256,2048]{1,0:T(8,128)(2,1)} %get-tuple-element.8), channel_id=1, source_target_pairs={{0,192},{64,0},{128,64},{192,128},{1,193},{65,1},{129,65},{193,129... | collective-permute-start | bytes 3145736 | tf_op jit(solution)/shard_map/ppermute | solution.py:22
  98.4 93.3 %collective-permute-start.3 = (bf16[512,1536]{0,1:T(8,128)(2,1)}, bf16[512,1536]{0,1:T(8,128)(2,1)}, u32[]{:S(2)}, u32[]{:S(2)}) collective-permute-start(bf16[512,1536]{0,1:T(8,128)(2,1)} %bitcast.47), channel_id=1, source_target_pairs={{0,16},{16,32},{32,48},{48,0},{1,17},{17,33},{33,49},{49,1},{2,18}... | collective-permute-start | bytes 4718600 | tf_op jit(solution)/shard_map/ppermute | solution.py:22
  99.9 97.8 %collective-permute-start.4 = (bf16[512,1536]{0,1:T(8,128)(2,1)}, bf16[512,1536]{0,1:T(8,128)(2,1)S(1)}, u32[]{:S(2)}, u32[]{:S(2)}) collective-permute-start(bf16[512,1536]{0,1:T(8,128)(2,1)} %bitcast.48), channel_id=1, source_target_pairs={{0,32},{16,48},{32,0},{48,16},{1,33},{17,49},{33,1},{49,17},{2,34}... | collective-permute-start | bytes 4718600 | tf_op jit(solution)/shard_map/ppermute | solution.py:22
  119.7 82.5 %collective-permute-start.5 = (bf16[512,1536]{0,1:T(8,128)(2,1)}, bf16[512,1536]{0,1:T(8,128)(2,1)}, u32[]{:S(2)}, u32[]{:S(2)}) collective-permute-start(bf16[512,1536]{0,1:T(8,128)(2,1)} %bitcast.49), channel_id=1, source_target_pairs={{0,48},{16,0},{32,16},{48,32},{1,49},{17,1},{33,17},{49,33},{2,50}... | collective-permute-start | bytes 4718600 | tf_op jit(solution)/shard_map/ppermute | solution.py:22
  187.6 2.4 copy-start.1
  209.5 3.4 %copy-start.3 = (bf16[3,3,512]{2,1,0:T(4,128)(2,1)S(1)}, bf16[3,3,512]{2,1,0:T(4,128)(2,1)}, u32[]{:S(2)}) copy-start(bf16[3,3,512]{2,1,0:T(4,128)(2,1)} %param.8) | copy-start | bytes 27652
  209.5 72.1 %copy-start.2 = (f32[512,16]{0,1:T(8,128)S(1)}, f32[512,16]{0,1:T(8,128)}, u32[]{:S(2)}) copy-start(f32[512,16]{0,1:T(8,128)} %param.9) | copy-start | bytes 98308
  209.7 54.4 %collective-permute-start.6 = (bf16[256,1536]{1,0:T(8,128)(2,1)S(1)}, bf16[256,1536]{1,0:T(8,128)(2,1)S(1)}, u32[]{:S(2)}, u32[]{:S(2)}) collective-permute-start(bf16[256,1536]{1,0:T(8,128)(2,1)S(1)} %get-tuple-element.11), channel_id=1, source_target_pairs={{0,192},{64,0},{128,64},{192,128},{1,193},{65,1},{129,65},{193,129... | collective-permute-start | bytes 2359304 | tf_op jit(solution)/shard_map/ppermute | solution.py:52
  210.0 54.1 %collective-permute-start.7 = (bf16[256,1536]{1,0:T(8,128)(2,1)S(1)}, bf16[256,1536]{1,0:T(8,128)(2,1)S(1)}, u32[]{:S(2)}, u32[]{:S(2)}) collective-permute-start(bf16[256,1536]{1,0:T(8,128)(2,1)S(1)} %get-tuple-element.13), channel_id=1, source_target_pairs={{0,128},{64,192},{128,0},{192,64},{1,129},{65,193},{129,1},{193,65... | collective-permute-start | bytes 2359304 | tf_op jit(solution)/shard_map/ppermute | solution.py:52
  211.0 66.9 %collective-permute-start.8 = (bf16[256,1536]{1,0:T(8,128)(2,1)S(1)}, bf16[256,1536]{1,0:T(8,128)(2,1)S(1)}, u32[]{:S(2)}, u32[]{:S(2)}) collective-permute-start(bf16[256,1536]{1,0:T(8,128)(2,1)S(1)} %get-tuple-element.12), channel_id=1, source_target_pairs={{0,64},{64,128},{128,192},{192,0},{1,65},{65,129},{129,193},{193,1... | collective-permute-start | bytes 2359304 | tf_op jit(solution)/shard_map/ppermute | solution.py:52
  278.2 9.2 %collective-permute-start.9 = (bf16[2,3,512]{2,0,1:T(2,128)(2,1)S(1)}, bf16[2,3,512]{2,0,1:T(2,128)(2,1)S(1)}, u32[]{:S(2)}, u32[]{:S(2)}) collective-permute-start(bf16[2,3,512]{2,0,1:T(2,128)(2,1)S(1)} %bitcast.57), channel_id=1, source_target_pairs={{0,16},{16,32},{32,48},{48,64},{64,80},{80,96},{96,112},{112,128},... | collective-permute-start | bytes 18440 | tf_op jit(solution)/shard_map/ppermute | solution.py:14
  289.8 5.2 %collective-permute-start.10 = (f32[512,16]{0,1:T(8,128)S(1)}, f32[512,16]{0,1:T(8,128)S(1)}, u32[]{:S(2)}, u32[]{:S(2)}) collective-permute-start(f32[512,16]{0,1:T(8,128)S(1)} %multiply_reduce_fusion), channel_id=1, source_target_pairs={{0,16},{16,32},{32,48},{48,0},{1,17},{17,33},{33,49},{49,1},{2,18}... | collective-permute-start | bytes 98312 | tf_op jit(solution)/shard_map/ppermute | solution.py:22
  289.9 5.5 %collective-permute-start.11 = (f32[512,16]{0,1:T(8,128)S(1)}, f32[512,16]{0,1:T(8,128)S(1)}, u32[]{:S(2)}, u32[]{:S(2)}) collective-permute-start(f32[512,16]{0,1:T(8,128)S(1)} %multiply_reduce_fusion), channel_id=1, source_target_pairs={{0,32},{16,48},{32,0},{48,16},{1,33},{17,49},{33,1},{49,17},{2,34}... | collective-permute-start | bytes 98312 | tf_op jit(solution)/shard_map/ppermute | solution.py:22
  290.5 5.6 %collective-permute-start.12 = (f32[512,16]{0,1:T(8,128)S(1)}, f32[512,16]{0,1:T(8,128)S(1)}, u32[]{:S(2)}, u32[]{:S(2)}) collective-permute-start(f32[512,16]{0,1:T(8,128)S(1)} %multiply_reduce_fusion), channel_id=1, source_target_pairs={{0,48},{16,0},{32,16},{48,32},{1,49},{17,1},{33,17},{49,33},{2,50}... | collective-permute-start | bytes 98312 | tf_op jit(solution)/shard_map/ppermute | solution.py:22
  296.2 8.4 %collective-permute-start.13 = (f32[4,512,16]{1,2,0:T(8,128)S(1)}, f32[4,512,16]{1,2,0:T(8,128)S(1)}, u32[]{:S(2)}, u32[]{:S(2)}) collective-permute-start(f32[4,512,16]{1,2,0:T(8,128)S(1)} %get-tuple-element.15), channel_id=1, source_target_pairs={{0,64},{64,128},{128,192},{192,0},{1,65},{65,129},{129,193},{193,1... | collective-permute-start | bytes 393224 | tf_op jit(solution)/shard_map/ppermute | solution.py:22
  297.2 8.8 %collective-permute-start.14 = (f32[4,512,16]{1,2,0:T(8,128)S(1)}, f32[4,512,16]{1,2,0:T(8,128)S(1)}, u32[]{:S(2)}, u32[]{:S(2)}) collective-permute-start(f32[4,512,16]{1,2,0:T(8,128)S(1)} %get-tuple-element.15), channel_id=1, source_target_pairs={{0,128},{64,192},{128,0},{192,64},{1,129},{65,193},{129,1},{193,65... | collective-permute-start | bytes 393224 | tf_op jit(solution)/shard_map/ppermute | solution.py:22
  300.3 7.9 %collective-permute-start.15 = (f32[4,512,16]{1,2,0:T(8,128)S(1)}, f32[4,512,16]{1,2,0:T(8,128)}, u32[]{:S(2)}, u32[]{:S(2)}) collective-permute-start(f32[4,512,16]{1,2,0:T(8,128)S(1)} %get-tuple-element.15), channel_id=1, source_target_pairs={{0,192},{64,0},{128,64},{192,128},{1,193},{65,1},{129,65},{193,129... | collective-permute-start | bytes 393224 | tf_op jit(solution)/shard_map/ppermute | solution.py:22
  300.5 8.7 %copy-start.5 = (f32[512,16]{0,1:T(8,128)S(1)}, f32[512,16]{0,1:T(8,128)}, u32[]{:S(2)}) copy-start(f32[512,16]{0,1:T(8,128)} %param.10) | copy-start | bytes 98308
  309.3 10.1 %copy-start.4 = (f32[512]{0:T(512)S(1)}, f32[512]{0:T(512)}, u32[]{:S(2)}) copy-start(f32[512]{0:T(512)} %param.11) | copy-start | bytes 6148
Sparse Core Ops, SparseCore 0:
  9.9 79.3 all-gather.1
where the time goes:
time: 327 us
  waiting for transfers between devices  244 us (75%)
  matrix products  29.6 us (9%)
  starting transfers between devices  24.3 us (7%)
  between operations  13.7 us (4%)
  other arithmetic  8.26 us (3%)
  local copies, waits for them, and re-layouts  7.05 us (2%)
    ppermute x12, waiting for transfers between devices, ring_sends(): received.append(lax.ppermute(pieces(k, position), axis, route))  91.4 us
    all_gather x1, waiting for transfers between devices, local(): gathered = lax.all_gather(tokens, 'ch', axis=1, tiled=True)  82 us
    ppermute x3, waiting for transfers between devices, local(): back = lax.ppermute(pieces[k].astype(jnp.bfloat16), 'zl', route)  64.9 us
    dot_general x4, matrix products, local(): jnp.dot(taken, weights[k], preferred_element_type=jnp.float32)  19.5 us
    ppermute x12, starting transfers between devices, ring_sends(): received.append(lax.ppermute(pieces(k, position), axis, route))  17.7 us
    dot_general x1, matrix products, local(): jnp.dot(lower_mask, scaled, precision=exact_mode)  10.1 us
  transfers between devices with their start and end apart: 17, of which 13 were waited for; matrix products, arithmetic and copies ran while one was open for 6% of the time, Pallas kernels for 0%

commit v1 on v0

--- a/solution.py
+++ b/solution.py
@@ -6,6 +6,14 @@
 
 exact_mode = lax.Precision.HIGHEST
 SEQ = ("zl", "x")
+
+
+def test_slices_on(point):
+    found_now = tuple((point for _ in range(jax.lax.psum(1, "ch"))))
+    met_up = jnp.stack(found_now)
+    parts_out = jax.lax.all_to_all(met_up, "ch", 0, 0)
+    mat_out = jnp.concatenate(parts_out, axis=1)
+    return mat_out
 
 
 def from_behind(block, axis, distance):
@@ -32,7 +40,7 @@
     me_x, me_z = (lax.axis_index("x"), lax.axis_index("zl"))
     flat_own = in_weight.reshape(feat_block, 3 * width_local)
     weights = [flat_own] + ring_sends(lambda k, p: flat_own, "x", across)
-    gathered = lax.all_gather(tokens, "ch", axis=1, tiled=True)
+    gathered = test_slices_on(tokens)
     chunk = gathered.shape[1] // down
 
     def chunk_for(k, p):

time: 327 us -> 340 us (1.040)
  between operations: 13.7 us -> 0.35 us
  starting transfers between devices: 24.3 us -> 37.6 us
  waiting for transfers between devices: 244 us -> 254 us
  local copies, waits for them, and re-layouts: 7.05 us -> 10.5 us
    all_to_all x0 -> x1, waiting for transfers between devices: none -> 99.2 us  [test_slices_on(): parts_out = jax.lax.all_to_all(met_up, 'ch', 0, 0)]
    all_gather x1 -> x0, waiting for transfers between devices: 82 us -> none  [local(): gathered = lax.all_gather(tokens, 'ch', axis=1, tiled=True)]
    all_to_all x0 -> x1, starting transfers between devices: none -> 10.4 us  [test_slices_on(): parts_out = jax.lax.all_to_all(met_up, 'ch', 0, 0)]
    ppermute x12, waiting for transfers between devices: 91.4 us -> 87.7 us  [ring_sends(): received.append(lax.ppermute(pieces(k, position), axis, route))]
  transfers between devices with their start and end apart: 17 -> 17, of which waited for: 13 -> 12; matrix products, arithmetic and copies ran while one was open for 6% -> 5% of each run, Pallas kernels for 0% -> 0%
where the time goes in v1:
time: 340 us
  waiting for transfers between devices  254 us (75%)
  starting transfers between devices  37.6 us (11%)
  matrix products  29.6 us (9%)
  local copies, waits for them, and re-layouts  10.5 us (3%)
  other arithmetic  8.38 us (2%)
    all_to_all x1, waiting for transfers between devices, test_slices_on(): parts_out = jax.lax.all_to_all(met_up, 'ch', 0, 0)  99.2 us
    ppermute x12, waiting for transfers between devices, ring_sends(): received.append(lax.ppermute(pieces(k, position), axis, route))  87.7 us
    ppermute x3, waiting for transfers between devices, local(): back = lax.ppermute(pieces[k].astype(jnp.bfloat16), 'zl', route)  63.3 us
    dot_general x4, matrix products, local(): jnp.dot(taken, weights[k], preferred_element_type=jnp.float32)  19.6 us
    ppermute x12, starting transfers between devices, ring_sends(): received.append(lax.ppermute(pieces(k, position), axis, route))  17.3 us
    all_to_all x1, starting transfers between devices, test_slices_on(): parts_out = jax.lax.all_to_all(met_up, 'ch', 0, 0)  10.4 us
    dot_general x1, matrix products, local(): jnp.dot(lower_mask, scaled, precision=exact_mode)  10.1 us
  transfers between devices with their start and end apart: 17, of which 12 were waited for; matrix products, arithmetic and copies ran while one was open for 5% of the time, Pallas kernels for 0%

profile of v1, /device:TPU:32, one launch (start us, length us, event | category | flops | bytes accessed | tf_op | source)
XLA Modules:
  0.0 340.1 jit_solution(8998982436846588221)
XLA Ops:
  1.1 2.4 stack.22
  3.5 10.4 %all-to-all-start = ((bf16[16,256,512]{1,2,0:T(8,128)(2,1)}), bf16[16,256,512]{1,2,0:T(8,128)(2,1)}, u32[]{:S(2)}, u32[]{:S(2)}) async-start(bf16[16,256,512]{1,2,0:T(8,128)(2,1)} %stack.22), calls=%async_computation | async-start | bytes 8388608 | tf_op jit(solution)/shard_map/all_to_all | solution.py:14
  13.9 99.2 %all-to-all-done = bf16[16,256,512]{1,2,0:T(8,128)(2,1)} async-done(((bf16[16,256,512]{1,2,0:T(8,128)(2,1)}), bf16[16,256,512]{1,2,0:T(8,128)(2,1)}, u32[]{:S(2)}, u32[]{:S(2)}) %all-to-all-start) | async-done | bytes 4194336 | tf_op jit(solution)/shard_map/all_to_all | solution.py:14
  113.1 4.1 %constant_dynamic-slice_fusion.3 = (bf16[256,2048]{0,1:T(8,128)(2,1)S(1)}, bf16[256,2048]{0,1:T(8,128)(2,1)}, bf16[256,2048]{0,1:T(8,128)(2,1)}, bf16[256,2048]{0,1:T(8,128)(2,1)}) fusion(bf16[256,8192]{0,1:T(8,128)(2,1)} %bitcast.4, s32[]{:T(128)S(6)} %select_n.86, s32[]{:T(128)S(6)} %select_n.92, s32[]{:T(128)S(6)} %select_n.90, s32[]{:T(128)S(6)} %select_n.88), kind=kLoop, calls=%fused_computation.55 | loop fusion | bytes 8388624 | tf_op jit(solution)/shard_map/dynamic_slice | solution.py:47
  122.9 2.7 collective-permute-start.4
  125.6 61.5 %collective-permute-done = bf16[256,2048]{0,1:T(8,128)(2,1)} collective-permute-done((bf16[256,2048]{0,1:T(8,128)(2,1)}, bf16[256,2048]{0,1:T(8,128)(2,1)}, u32[]{:S(2)}, u32[]{:S(2)}) %collective-permute-start) | collective-permute-done | bytes 1048608 | tf_op jit(solution)/shard_map/ppermute | solution.py:30
  187.1 2.8 collective-permute-start.5
  189.9 18.2 %collective-permute-done.1 = bf16[256,2048]{0,1:T(8,128)(2,1)} collective-permute-done((bf16[256,2048]{0,1:T(8,128)(2,1)}, bf16[256,2048]{0,1:T(8,128)(2,1)}, u32[]{:S(2)}, u32[]{:S(2)}) %collective-permute-start.1) | collective-permute-done | bytes 1048608 | tf_op jit(solution)/shard_map/ppermute | solution.py:30
  208.1 2.3 pad_maximum_fusion
  210.5 1.8 fusion.17
  212.3 5.9 %fusion.15 = f32[1024,1536]{1,0:T(8,128)} fusion(bf16[512,1536]{0,1:T(8,128)(2,1)} %collective-permute-done.3, bf16[1024,2048]{0,1:T(8,128)(2,1)S(1)} %pad_maximum_fusion, s32[]{:T(128)S(6)} %select_n.96), kind=kOutput, calls=%fused_computation.20 | convolution fusion | flops 1610612736 | bytes 8912900 | tf_op jit(solution)/shard_map/dot_general | solution.py:55
  218.2 4.5 %fusion.13 = f32[1024,1536]{1,0:T(8,128)} fusion(bf16[512,1536]{0,1:T(8,128)(2,1)S(1)} %collective-permute-done.4, bf16[1024,2048]{0,1:T(8,128)(2,1)S(1)} %pad_maximum_fusion, s32[]{:T(128)S(6)} %select_n.98), kind=kOutput, calls=%fused_computation.18 | convolution fusion | flops 1610612736 | bytes 8912900 | tf_op jit(solution)/shard_map/dot_general | solution.py:55
  222.7 7.3 %fusion.35 = (bf16[1024,1536]{1,0:T(8,128)(2,1)S(1)}, f32[1024,1536]{1,0:T(8,128)S(1)}) fusion(bf16[512,1536]{0,1:T(8,128)(2,1)} %collective-permute-done.5, bf16[1024,2048]{0,1:T(8,128)(2,1)S(1)} %pad_maximum_fusion, s32[]{:T(128)S(6)} %select_n.100, f32[1024,1536]{1,0:T(8,128)} %fusion.13, f32[1024,1536]{1,0:T(8,128)S(1)} %fusion.17, f32[1024,1536]{1,0:T(8,128)} %fusion.15), kind=kOutput, calls=%fused_computation.64 | convolution fusion | flops 1616904192 | bytes 30932996 | tf_op jit(solution)/shard_map/dot_general | solution.py:55
  230.3 3.5 %collective-permute-start.7 = (bf16[256,1536]{1,0:T(8,128)(2,1)S(1)}, bf16[256,1536]{1,0:T(8,128)(2,1)S(1)}, u32[]{:S(2)}, u32[]{:S(2)}) collective-permute-start(bf16[256,1536]{1,0:T(8,128)(2,1)S(1)} %get-tuple-element.13), channel_id=1, source_target_pairs={{0,128},{64,192},{128,0},{192,64},{1,129},{65,193},{129,1},{193,65... | collective-permute-start | bytes 2359304 | tf_op jit(solution)/shard_map/ppermute | solution.py:60
  233.8 2.8 collective-permute-start.8
  236.7 47.8 %collective-permute-done.6 = bf16[256,1536]{1,0:T(8,128)(2,1)S(1)} collective-permute-done((bf16[256,1536]{1,0:T(8,128)(2,1)S(1)}, bf16[256,1536]{1,0:T(8,128)(2,1)S(1)}, u32[]{:S(2)}, u32[]{:S(2)}) %collective-permute-start.6) | collective-permute-done | bytes 786464 | tf_op jit(solution)/shard_map/ppermute | solution.py:60
  284.4 15.6 %collective-permute-done.8 = bf16[256,1536]{1,0:T(8,128)(2,1)S(1)} collective-permute-done((bf16[256,1536]{1,0:T(8,128)(2,1)S(1)}, bf16[256,1536]{1,0:T(8,128)(2,1)S(1)}, u32[]{:S(2)}, u32[]{:S(2)}) %collective-permute-start.8) | collective-permute-done | bytes 786464 | tf_op jit(solution)/shard_map/ppermute | solution.py:60
  300.4 3.6 %collective-permute-start.9 = (bf16[2,3,512]{2,0,1:T(2,128)(2,1)S(1)}, bf16[2,3,512]{2,0,1:T(2,128)(2,1)S(1)}, u32[]{:S(2)}, u32[]{:S(2)}) collective-permute-start(bf16[2,3,512]{2,0,1:T(2,128)(2,1)S(1)} %bitcast.60), channel_id=1, source_target_pairs={{0,16},{16,32},{32,48},{48,64},{64,80},{80,96},{96,112},{112,128},... | collective-permute-start | bytes 18440 | tf_op jit(solution)/shard_map/ppermute | solution.py:22
  304.6 3.4 %collective-permute-done.9 = bf16[2,3,512]{2,0,1:T(2,128)(2,1)S(1)} collective-permute-done((bf16[2,3,512]{2,0,1:T(2,128)(2,1)S(1)}, bf16[2,3,512]{2,0,1:T(2,128)(2,1)S(1)}, u32[]{:S(2)}, u32[]{:S(2)}) %collective-permute-start.9) | collective-permute-done | bytes 6176 | tf_op jit(solution)/shard_map/ppermute | solution.py:22
  310.5 2.2 collective-permute-start.11
  316.8 2.6 collective-permute-start.13
  322.5 2.1 collective-permute-done.13
  324.6 2.8 collective-permute-done.14
  329.2 10.1 %multiply_reduce_fusion.1 = f32[256,512]{1,0:T(8,128)S(1)} fusion(f32[512,16]{0,1:T(8,128)S(1)} %exponential_multiply_fusion, f32[512,16]{0,1:T(8,128)S(1)} %neg.8, f32[512,16]{0,1:T(8,128)S(1)} %copy-done.5, f32[512,16,256]{2,1,0:T(8,128)S(1)} %bitcast.48), kind=kOutput, calls=%fused_computation.4 | convolution fusion | flops 6452871168 | bytes 9011200 | tf_op jit(solution)/shard_map/dot_general | solution.py:94
  (57 shorter events, 20.3 us)
Async XLA Ops:
  3.5 109.6 %all-to-all-start = ((bf16[16,256,512]{1,2,0:T(8,128)(2,1)}), bf16[16,256,512]{1,2,0:T(8,128)(2,1)}, u32[]{:S(2)}, u32[]{:S(2)}) async-start(bf16[16,256,512]{1,2,0:T(8,128)(2,1)} %stack.22), calls=%async_computation | async-start | bytes 8388608 | tf_op jit(solution)/shard_map/all_to_all | solution.py:14
  113.1 6.6 %copy-start = (bf16[512,3,512]{2,0,1:T(8,128)(2,1)S(1)}, bf16[512,3,512]{2,0,1:T(8,128)(2,1)}, u32[]{:S(2)}) copy-start(bf16[512,3,512]{2,0,1:T(8,128)(2,1)} %param.7) | copy-start | bytes 4718596
  117.2 69.9 %collective-permute-start = (bf16[256,2048]{0,1:T(8,128)(2,1)}, bf16[256,2048]{0,1:T(8,128)(2,1)}, u32[]{:S(2)}, u32[]{:S(2)}) collective-permute-start(bf16[256,2048]{0,1:T(8,128)(2,1)} %get-tuple-element.10), channel_id=1, source_target_pairs={{0,64},{64,128},{128,192},{192,0},{1,65},{65,129},{129,193},{193,1... | collective-permute-start | bytes 3145736 | tf_op jit(solution)/shard_map/ppermute | solution.py:30
  118.3 89.8 %collective-permute-start.1 = (bf16[256,2048]{0,1:T(8,128)(2,1)}, bf16[256,2048]{0,1:T(8,128)(2,1)}, u32[]{:S(2)}, u32[]{:S(2)}) collective-permute-start(bf16[256,2048]{0,1:T(8,128)(2,1)} %get-tuple-element.9), channel_id=1, source_target_pairs={{0,128},{64,192},{128,0},{192,64},{1,129},{65,193},{129,1},{193,65... | collective-permute-start | bytes 3145736 | tf_op jit(solution)/shard_map/ppermute | solution.py:30
  118.3 89.8 %collective-permute-start.2 = (bf16[256,2048]{0,1:T(8,128)(2,1)}, bf16[256,2048]{0,1:T(8,128)(2,1)}, u32[]{:S(2)}, u32[]{:S(2)}) collective-permute-start(bf16[256,2048]{0,1:T(8,128)(2,1)} %get-tuple-element.8), channel_id=1, source_target_pairs={{0,192},{64,0},{128,64},{192,128},{1,193},{65,1},{129,65},{193,129... | collective-permute-start | bytes 3145736 | tf_op jit(solution)/shard_map/ppermute | solution.py:30
  121.4 90.9 %collective-permute-start.3 = (bf16[512,1536]{0,1:T(8,128)(2,1)}, bf16[512,1536]{0,1:T(8,128)(2,1)}, u32[]{:S(2)}, u32[]{:S(2)}) collective-permute-start(bf16[512,1536]{0,1:T(8,128)(2,1)} %bitcast.50), channel_id=1, source_target_pairs={{0,16},{16,32},{32,48},{48,0},{1,17},{17,33},{33,49},{49,1},{2,18}... | collective-permute-start | bytes 4718600 | tf_op jit(solution)/shard_map/ppermute | solution.py:30
  122.9 95.4 %collective-permute-start.4 = (bf16[512,1536]{0,1:T(8,128)(2,1)}, bf16[512,1536]{0,1:T(8,128)(2,1)S(1)}, u32[]{:S(2)}, u32[]{:S(2)}) collective-permute-start(bf16[512,1536]{0,1:T(8,128)(2,1)} %bitcast.51), channel_id=1, source_target_pairs={{0,32},{16,48},{32,0},{48,16},{1,33},{17,49},{33,1},{49,17},{2,34}... | collective-permute-start | bytes 4718600 | tf_op jit(solution)/shard_map/ppermute | solution.py:30
  187.1 35.6 %collective-permute-start.5 = (bf16[512,1536]{0,1:T(8,128)(2,1)}, bf16[512,1536]{0,1:T(8,128)(2,1)}, u32[]{:S(2)}, u32[]{:S(2)}) collective-permute-start(bf16[512,1536]{0,1:T(8,128)(2,1)} %bitcast.52), channel_id=1, source_target_pairs={{0,48},{16,0},{32,16},{48,32},{1,49},{17,1},{33,17},{49,33},{2,50}... | collective-permute-start | bytes 4718600 | tf_op jit(solution)/shard_map/ppermute | solution.py:30
  208.1 2.4 copy-start.1
  230.1 6.6 %copy-start.3 = (bf16[3,3,512]{2,1,0:T(4,128)(2,1)S(1)}, bf16[3,3,512]{2,1,0:T(4,128)(2,1)}, u32[]{:S(2)}) copy-start(bf16[3,3,512]{2,1,0:T(4,128)(2,1)} %param.8) | copy-start | bytes 27652
  230.1 74.0 %copy-start.2 = (f32[512,16]{0,1:T(8,128)S(1)}, f32[512,16]{0,1:T(8,128)}, u32[]{:S(2)}) copy-start(f32[512,16]{0,1:T(8,128)} %param.9) | copy-start | bytes 98308
  230.2 54.2 %collective-permute-start.6 = (bf16[256,1536]{1,0:T(8,128)(2,1)S(1)}, bf16[256,1536]{1,0:T(8,128)(2,1)S(1)}, u32[]{:S(2)}, u32[]{:S(2)}) collective-permute-start(bf16[256,1536]{1,0:T(8,128)(2,1)S(1)} %get-tuple-element.11), channel_id=1, source_target_pairs={{0,192},{64,0},{128,64},{192,128},{1,193},{65,1},{129,65},{193,129... | collective-permute-start | bytes 2359304 | tf_op jit(solution)/shard_map/ppermute | solution.py:60
  230.3 54.1 %collective-permute-start.7 = (bf16[256,1536]{1,0:T(8,128)(2,1)S(1)}, bf16[256,1536]{1,0:T(8,128)(2,1)S(1)}, u32[]{:S(2)}, u32[]{:S(2)}) collective-permute-start(bf16[256,1536]{1,0:T(8,128)(2,1)S(1)} %get-tuple-element.13), channel_id=1, source_target_pairs={{0,128},{64,192},{128,0},{192,64},{1,129},{65,193},{129,1},{193,65... | collective-permute-start | bytes 2359304 | tf_op jit(solution)/shard_map/ppermute | solution.py:60
  233.8 66.2 %collective-permute-start.8 = (bf16[256,1536]{1,0:T(8,128)(2,1)S(1)}, bf16[256,1536]{1,0:T(8,128)(2,1)S(1)}, u32[]{:S(2)}, u32[]{:S(2)}) collective-permute-start(bf16[256,1536]{1,0:T(8,128)(2,1)S(1)} %get-tuple-element.12), channel_id=1, source_target_pairs={{0,64},{64,128},{128,192},{192,0},{1,65},{65,129},{129,193},{193,1... | collective-permute-start | bytes 2359304 | tf_op jit(solution)/shard_map/ppermute | solution.py:60
  300.4 7.6 %collective-permute-start.9 = (bf16[2,3,512]{2,0,1:T(2,128)(2,1)S(1)}, bf16[2,3,512]{2,0,1:T(2,128)(2,1)S(1)}, u32[]{:S(2)}, u32[]{:S(2)}) collective-permute-start(bf16[2,3,512]{2,0,1:T(2,128)(2,1)S(1)} %bitcast.60), channel_id=1, source_target_pairs={{0,16},{16,32},{32,48},{48,64},{64,80},{80,96},{96,112},{112,128},... | collective-permute-start | bytes 18440 | tf_op jit(solution)/shard_map/ppermute | solution.py:22
  310.4 5.2 %collective-permute-start.10 = (f32[512,16]{0,1:T(8,128)S(1)}, f32[512,16]{0,1:T(8,128)S(1)}, u32[]{:S(2)}, u32[]{:S(2)}) collective-permute-start(f32[512,16]{0,1:T(8,128)S(1)} %multiply_reduce_fusion), channel_id=1, source_target_pairs={{0,16},{16,32},{32,48},{48,0},{1,17},{17,33},{33,49},{49,1},{2,18}... | collective-permute-start | bytes 98312 | tf_op jit(solution)/shard_map/ppermute | solution.py:30
  310.5 5.5 %collective-permute-start.11 = (f32[512,16]{0,1:T(8,128)S(1)}, f32[512,16]{0,1:T(8,128)S(1)}, u32[]{:S(2)}, u32[]{:S(2)}) collective-permute-start(f32[512,16]{0,1:T(8,128)S(1)} %multiply_reduce_fusion), channel_id=1, source_target_pairs={{0,32},{16,48},{32,0},{48,16},{1,33},{17,49},{33,1},{49,17},{2,34}... | collective-permute-start | bytes 98312 | tf_op jit(solution)/shard_map/ppermute | solution.py:30
  312.7 4.1 %collective-permute-start.12 = (f32[512,16]{0,1:T(8,128)S(1)}, f32[512,16]{0,1:T(8,128)S(1)}, u32[]{:S(2)}, u32[]{:S(2)}) collective-permute-start(f32[512,16]{0,1:T(8,128)S(1)} %multiply_reduce_fusion), channel_id=1, source_target_pairs={{0,48},{16,0},{32,16},{48,32},{1,49},{17,1},{33,17},{49,33},{2,50}... | collective-permute-start | bytes 98312 | tf_op jit(solution)/shard_map/ppermute | solution.py:30
  316.8 7.8 %collective-permute-start.13 = (f32[4,512,16]{1,2,0:T(8,128)S(1)}, f32[4,512,16]{1,2,0:T(8,128)S(1)}, u32[]{:S(2)}, u32[]{:S(2)}) collective-permute-start(f32[4,512,16]{1,2,0:T(8,128)S(1)} %get-tuple-element.15), channel_id=1, source_target_pairs={{0,64},{64,128},{128,192},{192,0},{1,65},{65,129},{129,193},{193,1... | collective-permute-start | bytes 393224 | tf_op jit(solution)/shard_map/ppermute | solution.py:30
  319.4 8.0 %collective-permute-start.14 = (f32[4,512,16]{1,2,0:T(8,128)S(1)}, f32[4,512,16]{1,2,0:T(8,128)S(1)}, u32[]{:S(2)}, u32[]{:S(2)}) collective-permute-start(f32[4,512,16]{1,2,0:T(8,128)S(1)} %get-tuple-element.15), channel_id=1, source_target_pairs={{0,128},{64,192},{128,0},{192,64},{1,129},{65,193},{129,1},{193,65... | collective-permute-start | bytes 393224 | tf_op jit(solution)/shard_map/ppermute | solution.py:30
  319.4 8.6 %collective-permute-start.15 = (f32[4,512,16]{1,2,0:T(8,128)S(1)}, f32[4,512,16]{1,2,0:T(8,128)}, u32[]{:S(2)}, u32[]{:S(2)}) collective-permute-start(f32[4,512,16]{1,2,0:T(8,128)S(1)} %get-tuple-element.15), channel_id=1, source_target_pairs={{0,192},{64,0},{128,64},{192,128},{1,193},{65,1},{129,65},{193,129... | collective-permute-start | bytes 393224 | tf_op jit(solution)/shard_map/ppermute | solution.py:30
  321.2 7.9 %copy-start.5 = (f32[512,16]{0,1:T(8,128)S(1)}, f32[512,16]{0,1:T(8,128)}, u32[]{:S(2)}) copy-start(f32[512,16]{0,1:T(8,128)} %param.10) | copy-start | bytes 98308
  329.2 10.1 %copy-start.4 = (f32[512]{0:T(512)S(1)}, f32[512]{0:T(512)}, u32[]{:S(2)}) copy-start(f32[512]{0:T(512)} %param.11) | copy-start | bytes 6148
